TPU v7x, 256 devices: a whole 4x4x8 slice. The times are simulated.
256 devices in a mesh: req: 32 (over z_hi, y, core), tp: 8 (over x, z_lo).
Axes of the slice: x: 4, y: 4, z: 8 (z_hi: 4, z_lo: 2; z = z_hi * 2 + z_lo), core: 2. Of those that a mesh axis runs over, the one named last changes fastest.
Arguments:
- hidden_in: bfloat16 [4096, 5120], P('req', 'tp'), may hold values from -6 to 6
- norm_gain: bfloat16 [5120], P('tp'), may hold values from 0.099609375 to 1.8984375
- q_weight: bfloat16 [5120, 3072], P(None, 'tp'), may hold values from -0.078125 to 0.078125
- q_bias: bfloat16 [3072], P('tp'), may hold values from -4 to 4
- k_weight: bfloat16 [5120, 1024], P(None, 'tp'), may hold values from -0.125 to 0.125
- k_bias: bfloat16 [1024], P('tp'), may hold values from -5 to 5
- v_weight: bfloat16 [5120, 1024], P(None, 'tp'), may hold values from -0.3125 to 0.3125
- v_bias: bfloat16 [1024], P('tp'), may hold values from -10 to 10
- o_weight: bfloat16 [3072, 5120], P('tp'), may hold values from -0.3125 to 0.3125
- prefix_kv: bfloat16 [32768, 2, 1024], P('req', None, 'tp'), as said below
- suffix_len: int32 [32], P('req'), may hold values from 18 to 128, as said below
- req_prefix: int32 [32], P('req'), may hold values from 0 to 3, as said below
- block_owner: int32 [32], replicated, may hold values from 0 to 31, each once
Outputs:
- attn_out: bfloat16 [4096, 5120], P('req', 'tp')
Inputs may be any that keep to these rules, and one draw needn't show every extreme that they name: `suffix_len`: suffix tokens of each request; some request has exactly 128 and some exactly 18. `req_prefix`: every prefix is continued by exactly 8 requests. Block j of prefix p is held by req index block_owner[p * 8 + j]; each req index holds one block. `prefix_kv`: cached keys already carry the rotary embedding of their prefix positions.
All inputs are finite; a program needn't handle non-finite values.
Results may differ from a plain program's by a relative error of at most 0.022.
Values may be sent and summed in bfloat16 or wider, within the bound.
No kernel may reach another device: no remote copies, remote signals or barrier semaphores. Data moves between devices by JAX's collectives and lax.ppermute only.
A program may use at most 128 MiB of HBM per device.

v0:
```python
import jax
import jax.numpy as jnp
from jax import lax
from jax.sharding import PartitionSpec as P

HD = 128
NPREF = 4
THETA = 1000000.0
EPSILON = 1e-06


def rotate(heads, positions):
    half = HD // 2
    freqs = THETA ** (-(jnp.arange(half, dtype=jnp.float32) * 2.0) / HD)
    angles = positions.astype(jnp.float32)[:, None] * freqs[None, :]
    cosine = jnp.cos(angles)[:, None, :]
    sine = jnp.sin(angles)[:, None, :]
    first = heads[..., :half]
    second = heads[..., half:]
    return jnp.concatenate(
        [first * cosine - second * sine, second * cosine + first * sine], axis=-1
    )


def block_stats(grouped, keys, values, allowed):
    scores = jnp.einsum(
        "sghd,kgd->sghk", grouped, keys, preferred_element_type=jnp.float32
    ) * HD ** (-0.5)
    if allowed is not None:
        scores = jnp.where(allowed[:, None, None, :], scores, -jnp.inf)
    peak = jnp.max(scores, axis=-1)
    weights = jnp.exp(scores - peak[..., None])
    total = jnp.sum(weights, axis=-1)
    mixed = jnp.einsum(
        "sghk,kgd->sghd", weights.astype(jnp.bfloat16), values, preferred_element_type=jnp.float32
    )
    return (peak, total, mixed)


def combine(first, second):
    peak = jnp.maximum(first[0], second[0])
    left = jnp.exp(first[0] - peak)
    right = jnp.exp(second[0] - peak)
    total = first[1] * left + second[1] * right
    mixed = first[2] * left[..., None] + second[2] * right[..., None]
    return (peak, total, mixed)


def shards(
    hidden_in,
    norm_gain,
    q_weight,
    q_bias,
    k_weight,
    k_bias,
    v_weight,
    v_bias,
    o_weight,
    prefix_kv,
    suffix_len,
    req_prefix,
    block_owner,
):
    length = hidden_in.shape[0]
    devices = lax.axis_size("req")
    owned = devices // NPREF
    block = prefix_kv.shape[0]
    prefix_len = block * owned
    kv_heads = k_weight.shape[1] // HD
    q_heads = q_weight.shape[1] // HD
    group = q_heads // kv_heads
    full, gain = (
        lax.all_gather(hidden_in, "tp", axis=1, tiled=True),
        lax.all_gather(norm_gain, "tp", axis=0, tiled=True),
    )
    tokens = full.astype(jnp.float32)
    meansq = jnp.mean(tokens * tokens, axis=-1, keepdims=True)
    normed = (tokens * lax.rsqrt(meansq + EPSILON) * gain.astype(jnp.float32)).astype(jnp.bfloat16)
    positions = prefix_len + jnp.arange(length, dtype=jnp.int32)
    queries = jnp.dot(normed, q_weight, preferred_element_type=jnp.float32) + q_bias.astype(
        jnp.float32
    )
    queries = rotate(queries.reshape(length, q_heads, HD), positions).astype(jnp.bfloat16)
    queries = queries.reshape(length, kv_heads, group, HD)
    keys = jnp.dot(normed, k_weight, preferred_element_type=jnp.float32) + k_bias.astype(
        jnp.float32
    )
    keys = rotate(keys.reshape(length, kv_heads, HD), positions).astype(jnp.bfloat16)
    values = jnp.dot(normed, v_weight, preferred_element_type=jnp.float32) + v_bias.astype(
        jnp.float32
    )
    values = values.astype(jnp.bfloat16).reshape(length, kv_heads, HD)
    slot_index = jnp.arange(length, dtype=jnp.int32)
    causal = slot_index[None, :] <= slot_index[:, None]
    state = block_stats(queries, keys, values, causal)
    which = req_prefix[0]

    def advance(current, cached):
        return (combine(current, block_stats(queries, cached[:, 0], cached[:, 1], None)), None)

    everything = lax.all_gather(prefix_kv, "req", axis=0, tiled=True)
    stacked = everything.reshape(devices, block, 2, kv_heads, HD)
    owners = lax.dynamic_slice_in_dim(block_owner, which * owned, owned)
    chosen = jnp.take(stacked, owners, axis=0)
    state, unused = lax.scan(advance, state, chosen)
    peak, total, mixed = state
    context = (mixed / total[..., None]).astype(jnp.bfloat16).reshape(length, q_heads * HD)
    partial_value = jnp.dot(context, o_weight, preferred_element_type=jnp.float32)
    summed = lax.psum_scatter(
        partial_value.astype(jnp.bfloat16), "tp", scatter_dimension=1, tiled=True
    ).astype(jnp.float32)
    valid = slot_index < suffix_len[0]
    return jnp.where(valid[:, None], summed, jnp.float32(0.0)).astype(jnp.bfloat16)


def solution(mesh):
    placed = (
        P("req", "tp"),
        P("tp"),
        P(None, "tp"),
        P("tp"),
        P(None, "tp"),
        P("tp"),
        P(None, "tp"),
        P("tp"),
        P("tp", None),
        P("req", None, "tp"),
        P("req"),
        P("req"),
        P(),
    )
    return jax.shard_map(
        shards, mesh=mesh, in_specs=placed, out_specs=P("req", "tp"), check_vma=False
    )
```

profile of v0, /device:TPU:8, one launch (start us, length us, event | category | flops | bytes accessed | tf_op | source)
XLA Modules:
  0.0 277.1 jit_solution(18251878204632939527)
XLA Ops:
  6.6 0.0 all-gather.4.cloned.1.call-start
  6.6 0.7 all-gather.4.cloned.1.call-update
  7.3 0.0 all-gather.6.cloned.1.call-start
  7.3 1.9 copy.47
  9.3 0.0 reduce-scatter.4.cloned.1.call-start
  9.3 28.0 %all-gather = bf16[8,1,640]{2,1,0:T(2,128)(2,1)S(1)} all-gather(bf16[1,1,640]{2,1,0:T(2,128)(2,1)S(1)} %reshape.278), channel_id=1, replica_groups=mesh['req'=32,'tp'=8] {'tp'}, dimensions={0}, use_global_device_ids=true | all-gather | bytes 11520 | tf_op jit(solution)/shard_map/all_gather | solution.py:74
  38.2 0.1 compare_and_fusion
  38.3 0.3 multiply_cosine_fusion
  38.6 18.3 %all-gather.4.cloned.1.call-done = bf16[128,5120]{1,0:T(8,128)(2,1)} async-done(((bf16[128,640]{1,0:T(8,128)(2,1)}), bf16[128,5120]{1,0:T(8,128)(2,1)}) %all-gather.4.cloned.1.call-update) | async-done | bytes 1310736 | tf_op jit(solution)/shard_map/all_gather | solution.py:73
  56.9 1.6 fusion.15
  58.5 3.4 %convolution_add_fusion = f32[128,384]{1,0:T(8,128)S(1)} fusion(bf16[5120,384]{1,0:T(8,128)(2,1)} %param.17, f32[384]{0:T(512)S(1)} %convert_element_type.79, bf16[128,5120]{1,0:T(8,128)(2,1)} %all-gather.4.cloned.1.call-done, f32[5120]{0:T(1024)S(1)} %bitcast.155, f32[128]{0:T(128)S(1)} %add_rsqrt_fusion), kind=kOutput, calls=%fused_computation.36 | convolution fusion | flops 505987072 | bytes 5462016 | tf_op jit(solution)/shard_map/dot_general | solution.py:80
  62.0 0.1 copy.41
  62.1 0.1 copy.60
  62.3 0.1 copy.61
  62.4 0.1 subtract_convert_fusion
  62.5 0.1 pad_maximum_fusion
  62.6 0.7 copy-done.1
  63.3 2.1 fusion.20
  65.4 0.2 fusion.43
  65.6 0.3 fusion.50
  65.9 0.1 fusion.24
  65.9 0.8 convolution_bitcast_fusion.1
  66.7 96.2 %all-gather.6.cloned.1.call-done = bf16[32768,2,128]{2,0,1:T(8,128)(2,1)} async-done(((bf16[1024,2,128]{2,0,1:T(8,128)(2,1)}), bf16[32768,2,128]{2,0,1:T(8,128)(2,1)}) %all-gather.6.cloned.1.call-update) | async-done | bytes 16777232 | tf_op jit(solution)/shard_map/all_gather | solution.py:101
  162.9 13.8 %copy.48 = bf16[32,1024,2,128]{3,1,2,0:T(8,128)(2,1)} copy(bf16[32,1024,2,128]{3,1,0,2:T(8,128)(2,1)} %bitcast.145) | data formatting | bytes 33554432 | tf_op jit(solution)/shard_map/reshape | solution.py:102
  176.6 8.8 %gather_fusion = bf16[8,1024,2,128]{3,1,2,0:T(8,128)(2,1)} fusion(bf16[32,1024,2,128]{3,1,2,0:T(8,128)(2,1)} %copy.48, s32[1024]{0:T(1024)S(1)} %pad_clamp_fusion), kind=kCustom, calls=%fused_computation | custom fusion | bytes 8388640 | tf_op jit(solution)/shard_map/jit(_take)/gather | solution.py:104
  185.4 4.6 %fusion.14 = bf16[8,1024,2,1,128]{4,1,2,3,0:T(8,128)(2,1)} fusion(bf16[8,1024,2,128]{3,1,2,0:T(8,128)(2,1)} %gather_fusion, pred[8]{0:T(512)(128)(4,1)S(1)} %get-tuple-element.72), kind=kLoop, calls=%fused_computation.27 | loop fusion | flops 2097152 | bytes 8388616 | tf_op jit(solution)/shard_map/while | solution.py:105
  190.0 17.9 %while.14 = (s32[]{:T(128)}, f32[128,1,3]{0,2,1:T(4,128)S(1)}, f32[128,1,3]{0,2,1:T(4,128)S(1)}, f32[128,1,3,128]{0,3,2,1:T(8,128)S(1)}, bf16[8,1024,2,1,128]{4,...) while((s32[]{:T(128)}, f32[128,1,3]{0,2,1:T(4,128)S(1)}, f32[128,1,3]{0,2,1:T(4,128)S(1)}, ...), condition=%wide.region_6.7_spmd, body=%wide.region_3.0_spmd.sunk | while | flops 203835264 | bytes 6813777 | solution.py:105
  190.0 1.1 dynamic-slice_bitcast_fusion.2
  191.1 0.4 bitcast_reduce_fusion.2
  191.5 0.2 fusion.63
  191.7 0.5 fusion.65
  192.3 1.1 dynamic-slice_bitcast_fusion.2
  193.3 0.4 bitcast_reduce_fusion.2
  193.7 0.2 fusion.63
  194.0 0.5 fusion.65
  194.5 1.1 dynamic-slice_bitcast_fusion.2
  195.6 0.4 bitcast_reduce_fusion.2
  196.0 0.2 fusion.63
  196.2 0.5 fusion.65
  196.7 1.1 dynamic-slice_bitcast_fusion.2
  197.8 0.4 bitcast_reduce_fusion.2
  198.2 0.2 fusion.63
  198.5 0.5 fusion.65
  199.0 1.1 dynamic-slice_bitcast_fusion.2
  200.1 0.4 bitcast_reduce_fusion.2
  200.4 0.2 fusion.63
  200.7 0.5 fusion.65
  201.2 1.1 dynamic-slice_bitcast_fusion.2
  202.3 0.4 bitcast_reduce_fusion.2
  202.7 0.2 fusion.63
  202.9 0.5 fusion.65
  203.5 1.1 dynamic-slice_bitcast_fusion.2
  204.5 0.4 bitcast_reduce_fusion.2
  204.9 0.2 fusion.63
  205.2 0.5 fusion.65
  205.7 1.1 dynamic-slice_bitcast_fusion.2
  206.8 0.4 bitcast_reduce_fusion.2
  207.2 0.2 fusion.63
  207.4 0.5 fusion.65
  208.0 3.0 %convolution_convert_fusion = bf16[128,5120]{1,0:T(8,128)(2,1)S(1)} fusion(bf16[128,384]{0,1:T(8,128)(2,1)S(1)} %bitcast.150, bf16[384,5120]{1,0:T(8,128)(2,1)} %param.23), kind=kOutput, calls=%fused_computation.25 | convolution fusion | flops 503971840 | bytes 5341184 | tf_op jit(solution)/shard_map/dot_general | solution.py:108
  211.0 1.4 copy.58
  213.1 55.6 %reduce-scatter.4.cloned.1.call-done = bf16[640,128]{1,0:T(8,128)(2,1)} async-done(((bf16[5120,128]{1,0:T(8,128)(2,1)}), bf16[640,128]{1,0:T(8,128)(2,1)}) %reduce-scatter.4.cloned.1.call-update) | async-done | bytes 163856
  268.7 1.1 copy.59
  269.8 0.8 select_convert_fusion
  (52 shorter events, 0.4 us)
Async XLA Ops:
  6.5 59.4 %copy-start = (bf16[5120,128]{1,0:T(8,128)(2,1)S(1)}, bf16[5120,128]{1,0:T(8,128)(2,1)}, u32[]{:S(2)}) copy-start(bf16[5120,128]{1,0:T(8,128)(2,1)} %param.21) | copy-start | bytes 3932164
  6.5 2.8 %copy-start.2 = (bf16[640]{0:T(1024)(128)(2,1)S(1)}, bf16[640]{0:T(1024)(128)(2,1)}, u32[]{:S(2)}) copy-start(bf16[640]{0:T(1024)(128)(2,1)} %param.16) | copy-start | bytes 3844
  6.5 30.9 %copy-start.3 = (bf16[384]{0:T(512)(128)(2,1)S(1)}, bf16[384]{0:T(512)(128)(2,1)}, u32[]{:S(2)}) copy-start(bf16[384]{0:T(512)(128)(2,1)} %param.18) | copy-start | bytes 2308
  6.5 30.9 %copy-start.5 = (bf16[128]{0:T(256)(128)(2,1)S(1)}, bf16[128]{0:T(256)(128)(2,1)}, u32[]{:S(2)}) copy-start(bf16[128]{0:T(256)(128)(2,1)} %param.20) | copy-start | bytes 772
  6.5 30.9 %copy-start.6 = (bf16[128]{0:T(256)(128)(2,1)S(1)}, bf16[128]{0:T(256)(128)(2,1)}, u32[]{:S(2)}) copy-start(bf16[128]{0:T(256)(128)(2,1)} %param.22) | copy-start | bytes 772
  6.5 31.6 %copy-start.4 = (s32[32]{0:T(128)S(1)}, s32[32]{0:T(128)}, u32[]{:S(2)}) copy-start(s32[32]{0:T(128)} %param.27) | copy-start | bytes 388
  6.6 50.3 %all-gather.4.cloned.1.call-start = ((), (), s32[]{:S(2)}) async-start(), calls=%async_computation.1 | async-start | bytes 1474560 | tf_op jit(solution)/shard_map/all_gather | solution.py:73
  7.3 155.6 %all-gather.6.cloned.1.call-start = ((), (), s32[]{:S(2)}) async-start(), calls=%async_computation.2 | async-start | bytes 17301504 | tf_op jit(solution)/shard_map/all_gather | solution.py:101
  9.3 259.5 %reduce-scatter.4.cloned.1.call-start = ((), (), s32[]{:S(2)}) async-start(), calls=%async_computation.3 | async-start | bytes 1474560
  62.0 1.3 copy-start.1
Sparse Core Ops, SparseCore 0:
  9.2 47.6 all-gather.3
  59.5 103.3 all-gather.5
  212.6 56.1 reduce-scatter.3
where the time goes:
time: 278 us; the launch traced here: 277 us
  waiting for transfers between devices  171 us (62%)
  local copies, waits for them, and re-layouts  36.8 us (13%)
  blocking collectives  28 us (10%)
  matrix products  16.4 us (6%)
  between operations  14.6 us (5%)
  other arithmetic  9.93 us (4%)
    all_gather x1, waiting for transfers between devices, shards(): everything = lax.all_gather(prefix_kv, 'req', axis=0, tiled=True)  96.2 us
    unnamed x4, waiting for transfers between devices  56.4 us
    all_gather x1, blocking collectives, shards(): lax.all_gather(norm_gain, 'tp', axis=0, tiled=True)  28 us
    all_gather x1, waiting for transfers between devices, shards(): lax.all_gather(hidden_in, 'tp', axis=1, tiled=True)  18.3 us
    reshape x1, local copies, waits for them, and re-layouts, shards(): stacked = everything.reshape(devices, block, 2, kv_heads, HD)  13.8 us
    gather x1, local copies, waits for them, and re-layouts, shards(): chosen = jnp.take(stacked, owners, axis=0)  8.79 us
    squeeze x8, local copies, waits for them, and re-layouts, shards(): state, unused = lax.scan(advance, state, chosen)  8.64 us
  transfers between devices with their start and end apart: 3, of which 3 were waited for; matrix products, arithmetic and copies ran while one was open for 4% of the time, Pallas kernels for 0%

commit v1 on v0

--- a/solution.py
+++ b/solution.py
@@ -98,7 +98,10 @@
     def advance(current, cached):
         return (combine(current, block_stats(queries, cached[:, 0], cached[:, 1], None)), None)
 
-    everything = lax.all_gather(prefix_kv, "req", axis=0, tiled=True)
+    count = lax.axis_size("req")
+    parts = jnp.stack([prefix_kv for _ in range(count)])
+    parts = lax.all_to_all(parts, "req", split_axis=0, concat_axis=0)
+    everything = jnp.concatenate(parts, axis=0)
     stacked = everything.reshape(devices, block, 2, kv_heads, HD)
     owners = lax.dynamic_slice_in_dim(block_owner, which * owned, owned)
     chosen = jnp.take(stacked, owners, axis=0)

time: 278 us -> 537 us (1.93)
  blocking collectives: 28 us -> 406 us
  waiting for transfers between devices: 171 us -> 48.5 us
  starting transfers between devices: 0.12 us -> 12 us
  local copies, waits for them, and re-layouts: 36.8 us -> 28.5 us
    all_gather x1, blocking collectives: 28 us -> 406 us  [shards(): lax.all_gather(norm_gain, 'tp', axis=0, tiled=True)]
    all_gather x1 -> x0, waiting for transfers between devices: 96.2 us -> none  [shards(): everything = lax.all_gather(prefix_kv, 'req', axis=0, tiled=True)]
    all_gather x1, waiting for transfers between devices: 18.3 us -> 0.02 us  [shards(): lax.all_gather(hidden_in, 'tp', axis=1, tiled=True)]
    reshape x1 -> x0, local copies, waits for them, and re-layouts: 13.8 us -> none  [shards(): stacked = everything.reshape(devices, block, 2, kv_heads, HD)]
    all_to_all x0 -> x1, starting transfers between devices: none -> 11.9 us  [shards(): parts = lax.all_to_all(parts, 'req', split_axis=0, concat_axis=0)]
    unnamed x4 -> x3, waiting for transfers between devices: 56.4 us -> 48.5 us
    another operation x0 -> x1, local copies, waits for them, and re-layouts: none -> 6.17 us  [shards(): parts = jnp.stack([prefix_kv for _ in range(count)])]
  transfers between devices with their start and end apart: 3 -> 3, of which waited for: 3 -> 1; matrix products, arithmetic and copies ran while one was open for 4% -> 2% of each run, Pallas kernels for 0% -> 0%
where the time goes in v1:
time: 537 us; the launch traced here: 536 us
  blocking collectives  406 us (76%)
  waiting for transfers between devices  48.5 us (9%)
  local copies, waits for them, and re-layouts  28.5 us (5%)
  matrix products  16.5 us (3%)
  between operations  15 us (3%)
  starting transfers between devices  12 us (2%)
  other arithmetic  9.94 us (2%)
    all_gather x1, blocking collectives, shards(): lax.all_gather(norm_gain, 'tp', axis=0, tiled=True)  406 us
    unnamed x3, waiting for transfers between devices  48.5 us
    all_to_all x1, starting transfers between devices, shards(): parts = lax.all_to_all(parts, 'req', split_axis=0, concat_axis=0)  11.9 us
  transfers between devices with their start and end apart: 3, of which 1 were waited for; matrix products, arithmetic and copies ran while one was open for 2% of the time, Pallas kernels for 0%

profile of v1, /device:TPU:8, one launch (start us, length us, event | category | flops | bytes accessed | tf_op | source)
XLA Modules:
  0.0 536.5 jit_solution(6439189096720914906)
XLA Ops:
  6.5 1.2 copy.37
  7.8 6.2 %stack.2 = bf16[32,1024,2,128]{3,1,2,0:T(8,128)(2,1)} broadcast(bf16[1024,2,128]{2,0,1:T(8,128)(2,1)S(1)} %copy.37), dimensions={1,2,3} | broadcast | bytes 17301504 | tf_op jit(solution)/shard_map/stack | solution.py:102
  13.9 11.9 %all-to-all-start = ((bf16[32,1024,2,128]{3,1,2,0:T(8,128)(2,1)}), bf16[32,1024,2,128]{3,1,2,0:T(8,128)(2,1)}, u32[]{:S(2)}, u32[]{:S(2)}) async-start(bf16[32,1024,2,128]{3,1,2,0:T(8,128)(2,1)} %stack.2), calls=%async_computation | async-start | bytes 33554432 | tf_op jit(solution)/shard_map/all_to_all | solution.py:103
  25.9 0.0 all-gather.3.cloned.1.call-start
  25.9 0.7 all-gather.3.cloned.1.call-update
  26.6 0.0 reduce-scatter.4.cloned.1.call-start
  26.7 405.8 %all-gather = bf16[8,1,640]{2,1,0:T(2,128)(2,1)S(1)} all-gather(bf16[1,1,640]{2,1,0:T(2,128)(2,1)S(1)} %reshape.276), channel_id=1, replica_groups=mesh['req'=32,'tp'=8] {'tp'}, dimensions={0}, use_global_device_ids=true | all-gather | bytes 11520 | tf_op jit(solution)/shard_map/all_gather | solution.py:74
  433.2 0.1 compare_and_fusion
  433.3 0.3 multiply_cosine_fusion
  433.6 0.0 all-gather.3.cloned.1.call-done
  433.6 1.7 fusion.15
  435.3 3.4 convolution_add_fusion
  438.7 0.1 copy.31
  438.9 0.1 copy.49
  439.0 0.1 copy.50
  439.2 0.1 subtract_convert_fusion
  439.2 0.1 pad_maximum_fusion
  439.3 0.7 copy-done.1
  440.1 2.1 fusion.20
  442.1 0.2 fusion.43
  442.3 0.3 fusion.50
  442.6 0.1 fusion.24
  442.7 0.8 convolution_bitcast_fusion.1
  443.5 8.8 %gather_fusion = bf16[8,1024,2,128]{3,1,2,0:T(8,128)(2,1)} fusion(bf16[32,1024,2,128]{3,1,2,0:T(8,128)(2,1)} %all-to-all-done, s32[1024]{0:T(1024)S(1)} %pad_clamp_fusion), kind=kCustom, calls=%fused_computation | custom fusion | bytes 8388640 | tf_op jit(solution)/shard_map/jit(_take)/gather | solution.py:107
  452.3 4.6 fusion.14
  456.9 18.0 %while.14 = (s32[]{:T(128)}, f32[128,1,3]{0,2,1:T(4,128)S(1)}, f32[128,1,3]{0,2,1:T(4,128)S(1)}, f32[128,1,3,128]{0,3,2,1:T(8,128)S(1)}, bf16[8,1024,2,1,128]{4,...) while((s32[]{:T(128)}, f32[128,1,3]{0,2,1:T(4,128)S(1)}, f32[128,1,3]{0,2,1:T(4,128)S(1)}, ...), condition=%wide.region_6.7_spmd, body=%wide.region_3.0_spmd.sunk | while | flops 203835264 | bytes 6813777 | solution.py:108
  456.9 1.1 dynamic-slice_bitcast_fusion.2
  457.9 0.4 bitcast_reduce_fusion.2
  458.3 0.2 fusion.63
  458.6 0.5 fusion.65
  459.1 1.1 dynamic-slice_bitcast_fusion.2
  460.2 0.4 bitcast_reduce_fusion.2
  460.6 0.2 fusion.63
  460.8 0.5 fusion.65
  461.4 1.1 dynamic-slice_bitcast_fusion.2
  462.4 0.4 bitcast_reduce_fusion.2
  462.8 0.2 fusion.63
  463.1 0.5 fusion.65
  463.6 1.1 dynamic-slice_bitcast_fusion.2
  464.7 0.4 bitcast_reduce_fusion.2
  465.1 0.2 fusion.63
  465.3 0.5 fusion.65
  465.8 1.1 dynamic-slice_bitcast_fusion.2
  466.9 0.4 bitcast_reduce_fusion.2
  467.3 0.2 fusion.63
  467.6 0.5 fusion.65
  468.1 1.1 dynamic-slice_bitcast_fusion.2
  469.2 0.4 bitcast_reduce_fusion.2
  469.6 0.2 fusion.63
  469.8 0.5 fusion.65
  470.3 1.1 dynamic-slice_bitcast_fusion.2
  471.4 0.4 bitcast_reduce_fusion.2
  471.8 0.2 fusion.63
  472.1 0.5 fusion.65
  472.6 1.1 dynamic-slice_bitcast_fusion.2
  473.7 0.4 bitcast_reduce_fusion.2
  474.1 0.2 fusion.63
  474.3 0.5 fusion.65
  474.9 3.0 convolution_convert_fusion
  477.9 1.4 copy.47
  479.3 0.0 reduce-scatter.4.cloned.1.call-update
  480.0 47.8 %reduce-scatter.4.cloned.1.call-done = bf16[640,128]{1,0:T(8,128)(2,1)} async-done(((bf16[5120,128]{1,0:T(8,128)(2,1)}), bf16[640,128]{1,0:T(8,128)(2,1)}) %reduce-scatter.4.cloned.1.call-update) | async-done | bytes 163856
  527.8 1.1 copy.48
  528.8 0.8 select_convert_fusion
  (51 shorter events, 0.4 us)
Async XLA Ops:
  6.5 436.1 %copy-start = (bf16[5120,128]{1,0:T(8,128)(2,1)S(1)}, bf16[5120,128]{1,0:T(8,128)(2,1)}, u32[]{:S(2)}) copy-start(bf16[5120,128]{1,0:T(8,128)(2,1)} %param.21) | copy-start | bytes 3932164
  13.9 12.7 %copy-start.2 = (bf16[640]{0:T(1024)(128)(2,1)S(1)}, bf16[640]{0:T(1024)(128)(2,1)}, u32[]{:S(2)}) copy-start(bf16[640]{0:T(1024)(128)(2,1)} %param.16) | copy-start | bytes 3844
  13.9 418.5 %copy-start.3 = (bf16[384]{0:T(512)(128)(2,1)S(1)}, bf16[384]{0:T(512)(128)(2,1)}, u32[]{:S(2)}) copy-start(bf16[384]{0:T(512)(128)(2,1)} %param.18) | copy-start | bytes 2308
  13.9 418.5 %copy-start.5 = (bf16[128]{0:T(256)(128)(2,1)S(1)}, bf16[128]{0:T(256)(128)(2,1)}, u32[]{:S(2)}) copy-start(bf16[128]{0:T(256)(128)(2,1)} %param.20) | copy-start | bytes 772
  13.9 418.6 %copy-start.6 = (bf16[128]{0:T(256)(128)(2,1)S(1)}, bf16[128]{0:T(256)(128)(2,1)}, u32[]{:S(2)}) copy-start(bf16[128]{0:T(256)(128)(2,1)} %param.22) | copy-start | bytes 772
  13.9 419.2 %copy-start.4 = (s32[32]{0:T(128)S(1)}, s32[32]{0:T(128)}, u32[]{:S(2)}) copy-start(s32[32]{0:T(128)} %param.27) | copy-start | bytes 388
  13.9 429.5 %all-to-all-start = ((bf16[32,1024,2,128]{3,1,2,0:T(8,128)(2,1)}), bf16[32,1024,2,128]{3,1,2,0:T(8,128)(2,1)}, u32[]{:S(2)}, u32[]{:S(2)}) async-start(bf16[32,1024,2,128]{3,1,2,0:T(8,128)(2,1)} %stack.2), calls=%async_computation | async-start | bytes 33554432 | tf_op jit(solution)/shard_map/all_to_all | solution.py:103
  25.9 407.8 %all-gather.3.cloned.1.call-start = ((), (), s32[]{:S(2)}) async-start(), calls=%async_computation.2 | async-start | bytes 1474560 | tf_op jit(solution)/shard_map/all_gather | solution.py:73
  26.6 501.2 %reduce-scatter.4.cloned.1.call-start = ((), (), s32[]{:S(2)}) async-start(), calls=%async_computation.3 | async-start | bytes 1474560
  438.7 1.3 copy-start.1
Sparse Core Ops, SparseCore 0:
  28.5 169.3 all-gather.2
  479.5 48.2 reduce-scatter.3
